TPU v7x, 128 devices: a whole 4x4x4 slice. The times are simulated.
128 devices in a mesh: shard: 8 (over x, core), tensor: 16 (over z, y).
Axes of the slice: x: 4, y: 4, z: 4, core: 2. Of those that a mesh axis runs over, the one named last changes fastest.
Arguments:
- grad_square: bfloat16 [8, 768, 768], P(None, 'shard'), may hold values from -64 to 64
- grad_wide: bfloat16 [8, 2048, 768], P(None, 'shard'), may hold values from -64 to 64
- moment_square: float32 [8, 589824], P(None, ('shard', 'tensor')), may hold values from -6 to 6
- moment_wide: float32 [8, 1572864], P(None, ('shard', 'tensor')), may hold values from -6 to 6
Outputs:
- update_square: float32 [8, 768, 768], P(None, 'shard')
- update_wide: float32 [8, 2048, 768], P(None, 'shard')
- new_moment_square: float32 [8, 589824], P(None, ('shard', 'tensor'))
- new_moment_wide: float32 [8, 1572864], P(None, ('shard', 'tensor'))
All inputs are finite; a program needn't handle non-finite values.
Results may differ from a plain program's by a relative error of at most 0.0003.
Values sent between devices are 32-bit elements; how exact they have to be, the bound alone decides.
No kernel may reach another device: no remote copies, remote signals or barrier semaphores. Data moves between devices by JAX's collectives and lax.ppermute only.
A program may use at most 128 MiB of HBM per device.

v0:
```python
import math
import jax
import jax.numpy as jnp
from jax import lax
from jax.sharding import PartitionSpec as P

D = 768
FF = 2048
ITERS = 3
coef_a = 3.4445
coef_b = -4.775
coef_c = 2.0315
momentum_decay = 0.95
epsilon = 1e-07
PRECISION = lax.Precision.HIGH


def dot(x, y):
    return jnp.dot(x, y, precision=PRECISION, preferred_element_type=jnp.float32)


def gram_of(rows):
    return lax.dot_general(
        rows,
        rows,
        (((0,), (0,)), ((), ())),
        precision=PRECISION,
        preferred_element_type=jnp.float32,
    )


def own_rows(grad, member, tensor_count):
    row_piece = grad.shape[1] // tensor_count
    return lax.dynamic_slice_in_dim(grad, member * row_piece, row_piece, 1)


def shards(grad_square, grad_wide, moment_square, moment_wide):
    tensor_count = lax.axis_size("tensor")
    member = lax.axis_index("tensor")
    count_square, count_wide = (grad_square.shape[0], grad_wide.shape[0])
    assert count_square == count_wide and 2 * count_square == tensor_count
    flat_square = own_rows(grad_square, member, tensor_count).astype(jnp.float32)
    flat_wide = own_rows(grad_wide, member, tensor_count).astype(jnp.float32)
    new_square = momentum_decay * moment_square.reshape(flat_square.shape) + flat_square
    new_wide = momentum_decay * moment_wide.reshape(flat_wide.shape) + flat_wide
    look_square = flat_square + momentum_decay * new_square
    look_wide = flat_wide + momentum_decay * new_wide
    piece = look_wide.shape[1]
    pad = piece - look_square.shape[1]
    zeros = jnp.zeros((count_square, pad, look_wide.shape[2]), jnp.float32)
    send = jnp.concatenate([look_wide, look_square, zeros], axis=1).reshape(
        tensor_count, piece, look_wide.shape[2]
    )
    held = lax.all_to_all(send, "tensor", split_axis=0, concat_axis=0, tiled=True)
    rows = held.reshape(tensor_count * piece, held.shape[2])
    part = gram_of(rows)
    columns = part.shape[0]
    slab = jnp.zeros((8, columns), jnp.float32).at[0].set(jnp.sum(rows * rows, axis=0))
    packed = lax.psum(jnp.concatenate([part, slab], axis=0), "shard")
    gram = packed[:columns]
    eye = jnp.eye(columns, dtype=jnp.float32)
    total = jnp.sum(packed[columns])
    denom = jnp.sqrt(total) + epsilon
    current = rows / denom
    gram = lax.optimization_barrier(gram / (denom * denom))
    for iteration in range(ITERS - 1):
        square_gram = dot(gram, gram)
        mixer = coef_b * gram + coef_c * square_gram
        current = coef_a * current + dot(current, mixer)
        full = mixer + coef_a * eye
        gram = dot(full, dot(gram, full))
    is_square = member % 2 == 1
    scale = jnp.where(is_square, jnp.float32(math.sqrt(D)), jnp.float32(math.sqrt(FF)))

    def finish(block):
        side = dot(block, gram)
        return scale * (coef_a * block + (coef_b * side + coef_c * dot(side, gram)))

    square_piece = piece - pad
    split = (current.shape[0] + (piece - pad) * tensor_count) // 2
    head, tail = (finish(current[:split]), finish(current[split:]))
    update = jnp.concatenate([head, tail], axis=0)
    square_rows = update.reshape(tensor_count, piece, -1)[:, :square_piece]
    square_rows = square_rows.reshape(tensor_count * square_piece, -1)
    wide_rows = update.shape[0]
    chunk = (square_rows.shape[0] + wide_rows) // 2
    assert 2 * chunk == square_rows.shape[0] + wide_rows and chunk == split
    to_odd = [(2 * j, 2 * j + 1) for j in range(count_square)]
    handed = lax.ppermute(tail, "tensor", to_odd)
    mine = jnp.where(is_square, jnp.concatenate([handed, square_rows], axis=0), head)
    gathered = lax.all_gather(mine, "tensor", axis=0, tiled=True)
    gathered = gathered.reshape(count_square, 2 * chunk, update.shape[1])
    update_wide = gathered[:, :wide_rows]
    update_square = gathered[:, wide_rows:]
    return (
        update_square,
        update_wide,
        new_square.reshape(moment_square.shape),
        new_wide.reshape(moment_wide.shape),
    )


def solution(mesh):
    return jax.shard_map(
        shards,
        mesh=mesh,
        in_specs=(
            P(None, "shard", None),
            P(None, "shard", None),
            P(None, ("shard", "tensor")),
            P(None, ("shard", "tensor")),
        ),
        out_specs=(
            P(None, "shard", None),
            P(None, "shard", None),
            P(None, ("shard", "tensor")),
            P(None, ("shard", "tensor")),
        ),
        check_vma=False,
    )
```

profile of v0, /device:TPU:1, one launch (start us, length us, event | category | flops | bytes accessed | tf_op | source)
XLA Modules:
  0.0 228.9 jit_solution(7076943141954339419)
XLA Ops:
  7.2 0.0 copy-start
  7.2 0.0 all-reduce.3.cloned.1.call-start
  7.2 1.0 broadcast_multiply_fusion.1
  8.2 0.3 copy-done
  8.6 0.7 convert_add_fusion.3
  9.2 0.1 copy.12
  9.3 1.0 broadcast_multiply_fusion
  10.3 0.1 pad.11.clone
  10.4 1.1 fusion.20
  11.5 0.1 maximum_maximum_fusion
  11.6 21.9 %all_to_all.5 = f32[16,16,768]{2,1,0:T(8,128)S(1)} all-to-all(f32[16,16,768]{2,1,0:T(8,128)S(1)} %bitcast.34), channel_id=1, replica_groups=mesh['shard'=8,'tensor'=16] {'tensor'}, dimensions={0} | all-to-all | bytes 1572864 | tf_op jit(solution)/shard_map/all_to_all | solution.py:54
  33.5 0.1 multiply_reduce_fusion
  33.6 1.3 convolution_bitcast_fusion
  34.9 1.6 select_maximum_fusion
  36.5 0.0 all-reduce.3.cloned.1.call-update
  36.5 0.2 all-gather.2.cloned.1.call-start
  36.8 63.0 %all-reduce.3.cloned.1.call-done = f32[776,768]{1,0:T(8,128)} async-done(((f32[776,768]{1,0:T(8,128)}), f32[776,768]{1,0:T(8,128)}) %all-reduce.3.cloned.1.call-update) | async-done | bytes 2383888 | tf_op jit(solution)/shard_map/psum | solution.py:59
  99.8 1.3 slice_reduce_fusion
  101.8 1.8 slice_divide_fusion
  103.7 3.3 %multiply_add_fusion.1 = f32[768,768]{1,0:T(8,128)S(1)} fusion(f32[768,768]{1,0:T(8,128)S(1)} %slice_divide_fusion), kind=kOutput, calls=%fused_computation.7 | convolution fusion | flops 2719678464 | bytes 4718592 | tf_op jit(solution)/shard_map/dot_general | solution.py:19
  107.0 3.1 %fusion.1 = f32[768,768]{1,0:T(8,128)S(1)} fusion(f32[768,768]{1,0:T(8,128)S(1)} %slice_divide_fusion, f32[768,768]{1,0:T(8,128)S(1)} %multiply_add_fusion.1), kind=kOutput, calls=%fused_computation.9 | convolution fusion | flops 2719678464 | bytes 7077888 | tf_op jit(solution)/shard_map/dot_general | solution.py:19
  110.1 3.2 %fusion = f32[768,768]{1,0:T(8,128)S(1)} fusion(f32[768,768]{1,0:T(8,128)S(1)} %fusion.1, f32[768,768]{1,0:T(8,128)S(1)} %multiply_add_fusion.1), kind=kOutput, calls=%fused_computation.8 | convolution fusion | flops 2719678464 | bytes 7077888 | tf_op jit(solution)/shard_map/dot_general | solution.py:19
  113.3 0.1 broadcast_divide_fusion
  113.4 1.4 convolution_add_fusion.1
  114.8 3.5 %multiply_add_fusion = f32[768,768]{1,0:T(8,128)S(1)} fusion(f32[768,768]{1,0:T(8,128)S(1)} %fusion), kind=kOutput, calls=%fused_computation.5 | convolution fusion | flops 2719678464 | bytes 4718592 | tf_op jit(solution)/shard_map/dot_general | solution.py:19
  118.3 3.1 %fusion.3 = f32[768,768]{1,0:T(8,128)S(1)} fusion(f32[768,768]{1,0:T(8,128)S(1)} %fusion, f32[768,768]{1,0:T(8,128)S(1)} %multiply_add_fusion), kind=kOutput, calls=%fused_computation.11 | convolution fusion | flops 2719678464 | bytes 7077888 | tf_op jit(solution)/shard_map/dot_general | solution.py:19
  121.4 1.4 convolution_add_fusion
  122.8 3.2 %fusion.2 = f32[768,768]{1,0:T(8,128)S(1)} fusion(f32[768,768]{1,0:T(8,128)S(1)} %fusion.3, f32[768,768]{1,0:T(8,128)S(1)} %multiply_add_fusion), kind=kOutput, calls=%fused_computation.10 | convolution fusion | flops 2719678464 | bytes 7077888 | tf_op jit(solution)/shard_map/dot_general | solution.py:19
  126.0 0.9 fusion.21
  126.9 1.1 fusion.18
  128.0 0.9 fusion.17
  129.0 3.1 %collective-permute-start = (f32[80,768]{1,0:T(8,128)S(1)}, f32[80,768]{1,0:T(8,128)S(1)}, u32[]{:S(2)}, u32[]{:S(2)}) collective-permute-start(f32[80,768]{1,0:T(8,128)S(1)} %fusion.17), channel_id=1, source_target_pairs={{0,1},{2,3},{4,5},{6,7},{8,9},{10,11},{12,13},{14,15},{16,17},{18,... | collective-permute-start | bytes 737288 | tf_op jit(solution)/shard_map/ppermute | solution.py:89
  132.1 1.1 fusion.6
  133.3 0.1 pad_maximum_fusion
  133.4 1.8 collective-permute-done
  135.2 0.9 maximum_select_fusion
  136.1 0.0 all-gather.2.cloned.1.call-update
  136.1 1.0 copy.14
  137.1 75.8 %all-gather.2.cloned.1.call-done = f32[2816,768]{1,0:T(8,128)} async-done(((f32[176,768]{1,0:T(8,128)}), f32[2816,768]{1,0:T(8,128)}) %all-gather.2.cloned.1.call-update) | async-done | bytes 8650768 | tf_op jit(solution)/shard_map/all_gather | solution.py:91
  212.9 3.2 %slice.47 = f32[8,96,768]{2,1,0:T(8,128)} slice(f32[8,352,768]{2,1,0:T(8,128)} %bitcast.32), slice={[0:8], [256:352], [0:768]} | slice | bytes 4718592 | tf_op jit(solution)/shard_map/slice | solution.py:94
  216.1 5.9 %slice.48 = f32[8,256,768]{2,1,0:T(8,128)} slice(f32[8,352,768]{2,1,0:T(8,128)} %bitcast.33), slice={[0:8], [0:256], [0:768]} | slice | bytes 12582912 | tf_op jit(solution)/shard_map/slice | solution.py:93
  (5 shorter events, 0.1 us)
Async XLA Ops:
  7.2 1.3 copy-start
  7.2 92.6 %all-reduce.3.cloned.1.call-start = ((), (), s32[]{:S(2)}) async-start(), calls=%async_computation.1 | async-start | bytes 4767744 | tf_op jit(solution)/shard_map/psum | solution.py:59
  36.5 176.4 %all-gather.2.cloned.1.call-start = ((), (), s32[]{:S(2)}) async-start(), calls=%async_computation.2 | async-start | bytes 9191424 | tf_op jit(solution)/shard_map/all_gather | solution.py:91
  129.0 6.2 %collective-permute-start = (f32[80,768]{1,0:T(8,128)S(1)}, f32[80,768]{1,0:T(8,128)S(1)}, u32[]{:S(2)}, u32[]{:S(2)}) collective-permute-start(f32[80,768]{1,0:T(8,128)S(1)} %fusion.17), channel_id=1, source_target_pairs={{0,1},{2,3},{4,5},{6,7},{8,9},{10,11},{12,13},{14,15},{16,17},{18,... | collective-permute-start | bytes 737288 | tf_op jit(solution)/shard_map/ppermute | solution.py:89
Sparse Core Ops, SparseCore 0:
  36.6 63.1 all-reduce.2
  136.2 76.6 all-gather.1
where the time goes:
time: 229 us
  waiting for transfers between devices  141 us (62%)
  matrix products  27.6 us (12%)
  blocking collectives  21.9 us (10%)
  between operations  14.9 us (7%)
  local copies, waits for them, and re-layouts  10.7 us (5%)
  other arithmetic  9.75 us (4%)
  starting transfers between devices  3.38 us (1%)
    all_gather x1, waiting for transfers between devices, shards(): gathered = lax.all_gather(mine, 'tensor', axis=0, tiled=True)  75.8 us
    psum x1, waiting for transfers between devices, shards(): packed = lax.psum(jnp.concatenate([part, slab], axis=0), 'shard')  63 us
    dot_general x12, matrix products, dot(): jnp.dot(x, y, precision=PRECISION, preferred_element_type=jnp.float32)  26.3 us
    all_to_all x1, blocking collectives, shards(): lax.all_to_all(send, 'tensor', split_axis=0, concat_axis=0, tiled=True)  21.9 us
    slice x1, local copies, waits for them, and re-layouts, shards(): update_wide = gathered[:, :wide_rows]  5.94 us
  transfers between devices with their start and end apart: 3, of which 3 were waited for; matrix products, arithmetic and copies ran while one was open for 1% of the time, Pallas kernels for 0%

commit v1 on v0

--- a/solution.py
+++ b/solution.py
@@ -56,7 +56,7 @@
     part = gram_of(rows)
     columns = part.shape[0]
     slab = jnp.zeros((8, columns), jnp.float32).at[0].set(jnp.sum(rows * rows, axis=0))
-    packed = lax.psum(jnp.concatenate([part, slab], axis=0), "shard")
+    packed = jnp.sum(lax.all_gather(jnp.concatenate([part, slab], axis=0), "shard"), axis=0)
     gram = packed[:columns]
     eye = jnp.eye(columns, dtype=jnp.float32)
     total = jnp.sum(packed[columns])

time: 229 us -> 268 us (1.17)
  waiting for transfers between devices: 141 us -> 170 us
  other arithmetic: 9.75 us -> 19.1 us
    all_gather x0 -> x1, waiting for transfers between devices: none -> 93.3 us  [shards(): lax.all_gather(jnp.concatenate([part, slab], axis=0), 'shard')]
    psum x1 -> x0, waiting for transfers between devices: 63 us -> none  [shards(): packed = lax.psum(jnp.concatenate([part, slab], axis=0), 'shard')]
    reduce_sum x0 -> x1, other arithmetic: none -> 9.35 us  [shards(): jnp.sum(lax.all_gather(jnp.concatenate([part, slab], axis=0), 'shard'), a...]
    all_gather x1, waiting for transfers between devices: 75.8 us -> 73.1 us  [shards(): gathered = lax.all_gather(mine, 'tensor', axis=0, tiled=True)]
where the time goes in v1:
time: 268 us
  waiting for transfers between devices  170 us (63%)
  matrix products  27.8 us (10%)
  blocking collectives  21.9 us (8%)
  other arithmetic  19.1 us (7%)
  between operations  15 us (6%)
  local copies, waits for them, and re-layouts  10.5 us (4%)
  starting transfers between devices  3.38 us (1%)
    all_gather x1, waiting for transfers between devices, shards(): lax.all_gather(jnp.concatenate([part, slab], axis=0), 'shard')  93.3 us
    all_gather x1, waiting for transfers between devices, shards(): gathered = lax.all_gather(mine, 'tensor', axis=0, tiled=True)  73.1 us
    dot_general x12, matrix products, dot(): jnp.dot(x, y, precision=PRECISION, preferred_element_type=jnp.float32)  26.5 us
    all_to_all x1, blocking collectives, shards(): lax.all_to_all(send, 'tensor', split_axis=0, concat_axis=0, tiled=True)  21.9 us
    reduce_sum x1, other arithmetic, shards(): jnp.sum(lax.all_gather(jnp.concatenate([part, slab], axis=0), 'shard'), a...  9.35 us
    slice x1, local copies, waits for them, and re-layouts, shards(): update_wide = gathered[:, :wide_rows]  6.04 us
  transfers between devices with their start and end apart: 3, of which 3 were waited for; matrix products, arithmetic and copies ran while one was open for 1% of the time, Pallas kernels for 0%

profile of v1, /device:TPU:1, one launch (start us, length us, event | category | flops | bytes accessed | tf_op | source)
XLA Modules:
  0.0 267.9 jit_solution(14342977197574222625)
XLA Ops:
  7.2 0.0 copy-start
  7.2 0.0 all-gather.6.cloned.1.call-start
  7.2 1.1 broadcast_multiply_fusion
  8.4 0.9 broadcast_multiply_fusion.1
  9.3 0.0 copy-done
  9.3 0.7 convert_add_fusion.3
  10.0 0.1 copy.12
  10.1 0.1 pad.11.clone
  10.2 1.1 fusion.20
  11.3 0.1 maximum_maximum_fusion
  11.4 21.9 %all_to_all.5 = f32[16,16,768]{2,1,0:T(8,128)S(1)} all-to-all(f32[16,16,768]{2,1,0:T(8,128)S(1)} %bitcast.36), channel_id=1, replica_groups=mesh['shard'=8,'tensor'=16] {'tensor'}, dimensions={0} | all-to-all | bytes 1572864 | tf_op jit(solution)/shard_map/all_to_all | solution.py:54
  33.3 0.1 multiply_reduce_fusion
  33.4 1.3 convolution_bitcast_fusion
  34.7 1.6 select_maximum_fusion
  36.2 0.0 all-gather.6.cloned.1.call-update
  36.3 0.2 all-gather.4.cloned.1.call-start
  36.5 93.3 %all-gather.6.cloned.1.call-done = f32[6208,768]{1,0:T(8,128)} async-done(((f32[776,768]{1,0:T(8,128)}), f32[6208,768]{1,0:T(8,128)}) %all-gather.6.cloned.1.call-update) | async-done | bytes 19070992 | tf_op jit(solution)/shard_map/all_gather | solution.py:59
  129.9 9.3 %reduce_sum.28 = f32[776,768]{1,0:T(8,128)} reduce(f32[8,776,768]{2,1,0:T(8,128)} %bitcast.33, f32[]{:T(128)} %constant.75.clone.1), dimensions={0}, to_apply=%region_1.0 | reduce | flops 4171776 | bytes 21454852 | tf_op jit(solution)/shard_map/reduce_sum | solution.py:59
  139.2 1.3 slice_reduce_fusion
  141.2 1.8 slice_divide_fusion
  143.1 3.3 %multiply_add_fusion.1 = f32[768,768]{1,0:T(8,128)S(1)} fusion(f32[768,768]{1,0:T(8,128)S(1)} %slice_divide_fusion), kind=kOutput, calls=%fused_computation.7 | convolution fusion | flops 2719678464 | bytes 4718592 | tf_op jit(solution)/shard_map/dot_general | solution.py:19
  146.4 3.1 %fusion.1 = f32[768,768]{1,0:T(8,128)S(1)} fusion(f32[768,768]{1,0:T(8,128)S(1)} %slice_divide_fusion, f32[768,768]{1,0:T(8,128)S(1)} %multiply_add_fusion.1), kind=kOutput, calls=%fused_computation.9 | convolution fusion | flops 2719678464 | bytes 7077888 | tf_op jit(solution)/shard_map/dot_general | solution.py:19
  149.5 0.1 broadcast_divide_fusion
  149.6 1.4 convolution_add_fusion.1
  151.0 3.4 %fusion = f32[768,768]{1,0:T(8,128)S(1)} fusion(f32[768,768]{1,0:T(8,128)S(1)} %fusion.1, f32[768,768]{1,0:T(8,128)S(1)} %multiply_add_fusion.1), kind=kOutput, calls=%fused_computation.8 | convolution fusion | flops 2719678464 | bytes 7077888 | tf_op jit(solution)/shard_map/dot_general | solution.py:19
  154.4 3.3 %multiply_add_fusion = f32[768,768]{1,0:T(8,128)S(1)} fusion(f32[768,768]{1,0:T(8,128)S(1)} %fusion), kind=kOutput, calls=%fused_computation.5 | convolution fusion | flops 2719678464 | bytes 4718592 | tf_op jit(solution)/shard_map/dot_general | solution.py:19
  157.7 3.1 %fusion.3 = f32[768,768]{1,0:T(8,128)S(1)} fusion(f32[768,768]{1,0:T(8,128)S(1)} %fusion, f32[768,768]{1,0:T(8,128)S(1)} %multiply_add_fusion), kind=kOutput, calls=%fused_computation.11 | convolution fusion | flops 2719678464 | bytes 7077888 | tf_op jit(solution)/shard_map/dot_general | solution.py:19
  160.8 1.4 convolution_add_fusion
  162.2 3.2 %fusion.2 = f32[768,768]{1,0:T(8,128)S(1)} fusion(f32[768,768]{1,0:T(8,128)S(1)} %fusion.3, f32[768,768]{1,0:T(8,128)S(1)} %multiply_add_fusion), kind=kOutput, calls=%fused_computation.10 | convolution fusion | flops 2719678464 | bytes 7077888 | tf_op jit(solution)/shard_map/dot_general | solution.py:19
  165.4 0.9 fusion.21
  166.3 1.1 fusion.18
  167.4 1.2 fusion.17
  168.6 3.1 %collective-permute-start = (f32[80,768]{1,0:T(8,128)S(1)}, f32[80,768]{1,0:T(8,128)S(1)}, u32[]{:S(2)}, u32[]{:S(2)}) collective-permute-start(f32[80,768]{1,0:T(8,128)S(1)} %fusion.17), channel_id=1, source_target_pairs={{0,1},{2,3},{4,5},{6,7},{8,9},{10,11},{12,13},{14,15},{16,17},{18,... | collective-permute-start | bytes 737288 | tf_op jit(solution)/shard_map/ppermute | solution.py:89
  171.8 1.1 fusion.6
  172.9 0.1 pad_maximum_fusion
  173.1 3.7 %collective-permute-done = f32[80,768]{1,0:T(8,128)S(1)} collective-permute-done((f32[80,768]{1,0:T(8,128)S(1)}, f32[80,768]{1,0:T(8,128)S(1)}, u32[]{:S(2)}, u32[]{:S(2)}) %collective-permute-start) | collective-permute-done | bytes 245792 | tf_op jit(solution)/shard_map/ppermute | solution.py:89
  176.8 0.9 maximum_select_fusion
  177.6 0.0 all-gather.4.cloned.1.call-update
  177.7 1.0 copy.14
  178.6 73.1 %all-gather.4.cloned.1.call-done = f32[2816,768]{1,0:T(8,128)} async-done(((f32[176,768]{1,0:T(8,128)}), f32[2816,768]{1,0:T(8,128)}) %all-gather.4.cloned.1.call-update) | async-done | bytes 8650768 | tf_op jit(solution)/shard_map/all_gather | solution.py:91
  251.7 0.0 copy-start.1
  251.8 6.0 %slice.48 = f32[8,256,768]{2,1,0:T(8,128)} slice(f32[8,352,768]{2,1,0:T(8,128)} %bitcast.34), slice={[0:8], [0:256], [0:768]} | slice | bytes 12582912 | tf_op jit(solution)/shard_map/slice | solution.py:93
  257.8 3.2 %slice.47 = f32[8,96,768]{2,1,0:T(8,128)} slice(f32[8,352,768]{2,1,0:T(8,128)} %bitcast.35), slice={[0:8], [256:352], [0:768]} | slice | bytes 4718592 | tf_op jit(solution)/shard_map/slice | solution.py:94
  261.0 0.0 copy-done.1
  (5 shorter events, 0.1 us)
Async XLA Ops:
  7.2 2.1 copy-start
  7.2 122.7 %all-gather.6.cloned.1.call-start = ((), (), s32[]{:S(2)}) async-start(), calls=%async_computation.2 | async-start | bytes 21454848 | tf_op jit(solution)/shard_map/all_gather | solution.py:59
  36.3 215.5 %all-gather.4.cloned.1.call-start = ((), (), s32[]{:S(2)}) async-start(), calls=%async_computation.1 | async-start | bytes 9191424 | tf_op jit(solution)/shard_map/all_gather | solution.py:91
  168.6 8.1 %collective-permute-start = (f32[80,768]{1,0:T(8,128)S(1)}, f32[80,768]{1,0:T(8,128)S(1)}, u32[]{:S(2)}, u32[]{:S(2)}) collective-permute-start(f32[80,768]{1,0:T(8,128)S(1)} %fusion.17), channel_id=1, source_target_pairs={{0,1},{2,3},{4,5},{6,7},{8,9},{10,11},{12,13},{14,15},{16,17},{18,... | collective-permute-start | bytes 737288 | tf_op jit(solution)/shard_map/ppermute | solution.py:89
  251.7 9.3 %copy-start.1 = (bf16[8,96,768]{2,1,0:T(8,128)(2,1)S(1)}, bf16[8,96,768]{2,1,0:T(8,128)(2,1)}, u32[]{:S(2)}) copy-start(bf16[8,96,768]{2,1,0:T(8,128)(2,1)} %param.6) | copy-start | bytes 3538948
Sparse Core Ops, SparseCore 0:
  36.4 93.4 all-gather.5
  177.8 73.9 all-gather.3
